TPU v7x, 256 devices: a whole 4x4x8 slice. The times are simulated.
256 devices in a mesh: seq: 16 (over y_lo, z), tm: 8 (over x, core), dp: 2 (over y_hi).
Axes of the slice: x: 4, y: 4 (y_hi: 2, y_lo: 2; y = y_hi * 2 + y_lo), z: 8, core: 2. Of those that a mesh axis runs over, the one named last changes fastest.
Arguments:
- queries: bfloat16 [16384, 8, 128], P(('dp', 'seq'), 'tm'), parts along dimension 0, may hold values from -6 to 6
- keys: bfloat16 [16384, 8, 128], P(('dp', 'seq'), 'tm'), parts along dimension 0, may hold values from -6 to 6
- values: bfloat16 [16384, 8, 128], P(('dp', 'seq'), 'tm'), parts along dimension 0, may hold values from -6 to 6
- token_cell: int32 [512], P('seq'), may hold values from 0 to 511, each once
- head_weight: bfloat16 [8, 128, 384], P('tm'), may hold values from -2 to 2
- norm_gain: float32 [384], replicated, may hold values from 0.1 to 1.9
- time_weight: bfloat16 [3, 384, 768], replicated, may hold values from -0.1875 to 0.1875
- frame_clip: int32 [32], P('dp'), parts along dimension 0, may hold values from 0 to 2, never falling along the last dimension, each value on 1 to 8 neighbouring positions
- cotangent: bfloat16 [32, 512, 768], P(('dp', 'tm'), 'seq'), parts along dimension 0, may hold values from -6 to 6
Outputs:
- grad_queries: bfloat16 [16384, 8, 128], P(('dp', 'seq'), 'tm'), parts along dimension 0
- grad_keys: bfloat16 [16384, 8, 128], P(('dp', 'seq'), 'tm'), parts along dimension 0
- grad_values: bfloat16 [16384, 8, 128], P(('dp', 'seq'), 'tm'), parts along dimension 0
There are 2 independent parts, one for each index of `dp`. A program takes and returns all parts, laid end to end along the dimension named above; an argument that names none is the same for every part. Nothing has to cross between parts.
Inputs may be any that keep to these rules, and one draw needn't show every extreme that they name: `token_cell`: a permutation of the 512 cells. `frame_clip`: never falls along the frames.
All inputs are finite; a program needn't handle non-finite values.
Results may differ from a plain program's by a relative error of at most 0.023.
Values may be sent and summed in bfloat16 or wider, within the bound.
No kernel may reach another device: no remote copies, remote signals or barrier semaphores. Data moves between devices by JAX's collectives and lax.ppermute only.
A program may use at most 64 MiB of HBM per device.

v0:
```python
import math
import jax
import jax.numpy as jnp
from jax import lax
from jax.sharding import PartitionSpec as P

HD = 128
GRID_W = 32


def shifted(value, axis, steps):
    count = lax.axis_size(axis)
    initial, last = (max(0, -steps), min(count, count - steps))
    return lax.ppermute(value, axis, [(source, source + steps) for source in range(initial, last)])


def frequencies(pair_count):
    return 1.0 / 10000.0 ** (jnp.arange(pair_count, dtype=jnp.float32) / pair_count)


def rope_tables(frame_pos, cell_ids):
    pair_count = HD // 2
    part_side = pair_count // 3
    part_time = pair_count - 2 * part_side
    grid_row = (cell_ids // GRID_W).astype(jnp.float32)
    grid_col = (cell_ids % GRID_W).astype(jnp.float32)
    angles = jnp.concatenate(
        [
            frame_pos.astype(jnp.float32)[:, None] * frequencies(part_time)[None, :],
            grid_row[:, None] * frequencies(part_side)[None, :],
            grid_col[:, None] * frequencies(part_side)[None, :],
        ],
        axis=1,
    )
    return (jnp.cos(angles), jnp.sin(angles))


def rotate(vectors, cos_table, sin_table, direction):
    layout = vectors.shape
    paired = vectors.reshape(layout[:-1] + (layout[-1] // 2, 2))
    former = paired[..., 0]
    latter = paired[..., 1]
    out_former = former * cos_table - direction * latter * sin_table
    out_latter = direction * former * sin_table + latter * cos_table
    return jnp.stack([out_former, out_latter], axis=-1).reshape(layout)


def tap_mask(frame_clip):
    frame_total = frame_clip.shape[0]
    frame_ids = jnp.arange(frame_total, dtype=jnp.int32)
    columns = []
    for offset in range(3):
        target = frame_ids + offset
        inside = target < frame_total
        same_clip = frame_clip[jnp.minimum(target, frame_total - 1)] == frame_clip
        columns.append(jnp.logical_and(inside, same_clip).astype(jnp.float32))
    return jnp.stack(columns, axis=1)


def cross(left, right):
    return lax.dot_general(
        left, right, (((1,), (1,)), ((), ())), preferred_element_type=jnp.float32
    )


def inner(left, right):
    return lax.dot_general(
        left, right, (((0,), (0,)), ((), ())), preferred_element_type=jnp.float32
    )


def on_device(
    queries, keys, values, token_cell, head_weight, norm_gain, time_weight, frame_clip, cotangent
):
    score_scale = HD ** (-0.5)
    tok_local = queries.shape[0]
    slab_cells = token_cell.shape[0]
    span_frames = cotangent.shape[0]
    channels = head_weight.shape[2]
    frame_pos = jnp.arange(tok_local, dtype=jnp.int32) // slab_cells
    cell_ids = jnp.tile(token_cell, tok_local // slab_cells)
    cos_table, sin_table = rope_tables(frame_pos, cell_ids)
    rot_q = rotate(queries[:, 0, :].astype(jnp.float32), cos_table, sin_table, 1.0).astype(
        jnp.bfloat16
    )
    rot_k = rotate(keys[:, 0, :].astype(jnp.float32), cos_table, sin_table, 1.0).astype(
        jnp.bfloat16
    )
    plain_v = values[:, 0, :]
    keys_all, values_all = (
        lax.all_gather(rot_k, "seq", axis=0, tiled=True),
        lax.all_gather(plain_v, "seq", axis=0, tiled=True),
    )
    total_tokens = keys_all.shape[0]
    key_block = math.gcd(total_tokens, 1024)
    block_count = total_tokens // key_block

    def forward_step(block_id, state):
        running_top, running_total, running_sum = state
        key_piece = lax.dynamic_slice_in_dim(keys_all, block_id * key_block, key_block, 0)
        value_piece = lax.dynamic_slice_in_dim(values_all, block_id * key_block, key_block, 0)
        scores = cross(rot_q, key_piece) * score_scale
        new_top = jnp.maximum(running_top, jnp.max(scores, axis=1))
        factor = jnp.exp(running_top - new_top)
        weights = jnp.exp(scores - new_top[:, None])
        running_total = running_total * factor + jnp.sum(weights, axis=1)
        running_sum = running_sum * factor[:, None] + jnp.dot(
            weights.astype(jnp.bfloat16), value_piece, preferred_element_type=jnp.float32
        )
        return (new_top, running_total, running_sum)

    start_state = (
        jnp.full((tok_local,), -1e30, jnp.float32),
        jnp.zeros((tok_local,), jnp.float32),
        jnp.zeros((tok_local, HD), jnp.float32),
    )
    row_top, row_total, summed = lax.fori_loop(0, block_count, forward_step, start_state)
    attended = (summed / row_total[:, None]).astype(jnp.bfloat16)
    log_total = row_top + jnp.log(row_total)
    span_rows = span_frames * slab_cells
    mixed = (
        lax.psum_scatter(
            jnp.dot(attended, head_weight[0], preferred_element_type=jnp.float32).astype(
                jnp.bfloat16
            ),
            "tm",
            scatter_dimension=0,
            tiled=True,
        )
        .astype(jnp.float32)
        .reshape(span_frames, slab_cells, channels)
    )
    inverse = lax.rsqrt(jnp.mean(mixed * mixed, axis=2, keepdims=True) + 1e-06)
    normed = mixed * inverse * norm_gain
    mask_table = tap_mask(frame_clip)
    first_frame = lax.axis_index("tm") * span_frames
    local_mask = lax.dynamic_slice_in_dim(mask_table, first_frame, span_frames, 0)
    following = shifted(cotangent, "tm", -1)
    extended = jnp.concatenate([cotangent, following], axis=0)
    grad_act = jnp.zeros((span_frames, slab_cells, channels), jnp.float32)
    for offset in range(3):
        term = jnp.einsum(
            "fco,io->fci",
            extended[offset : offset + span_frames],
            time_weight[offset],
            preferred_element_type=jnp.float32,
        )
        grad_act = grad_act + local_mask[:, offset][:, None, None] * term
    sigmoid_n = jax.nn.sigmoid(normed)
    grad_normed = grad_act * sigmoid_n * (1.0 + normed * (1.0 - sigmoid_n))
    gained = grad_normed * norm_gain
    grad_mixed = (
        inverse * gained
        - inverse * inverse * inverse * mixed * jnp.mean(gained * mixed, axis=2, keepdims=True)
    ).astype(jnp.bfloat16)
    grad_mixed = grad_mixed.reshape(span_rows, channels)
    grad_out = cross(lax.all_gather(grad_mixed, "tm", axis=0, tiled=True), head_weight[0]).astype(
        jnp.bfloat16
    )
    row_delta = jnp.sum(grad_out.astype(jnp.float32) * attended.astype(jnp.float32), axis=1)

    def score_block(block_id):
        key_piece = lax.dynamic_slice_in_dim(keys_all, block_id * key_block, key_block, 0)
        value_piece = lax.dynamic_slice_in_dim(values_all, block_id * key_block, key_block, 0)
        scores = cross(rot_q, key_piece) * score_scale
        weights = jnp.exp(scores - log_total[:, None])
        grad_w = cross(grad_out, value_piece)
        grad_s = (weights * (grad_w - row_delta[:, None])).astype(jnp.bfloat16)
        return (key_piece, weights, grad_s)

    def query_step(block_id, grad_q):
        key_piece, weights, grad_s = score_block(block_id)
        return grad_q + jnp.dot(grad_s, key_piece, preferred_element_type=jnp.float32) * score_scale

    grad_q = lax.fori_loop(0, block_count, query_step, jnp.zeros((tok_local, HD), jnp.float32))
    fold_start = (jnp.zeros((tok_local, HD), jnp.float32), jnp.zeros((tok_local, HD), jnp.float32))
    wide_q = rot_q.astype(jnp.float32)
    wide_grad = grad_out.astype(jnp.float32)
    piece_q = lax.all_gather(wide_q, "seq", axis=0, tiled=True)
    piece_grad = lax.all_gather(wide_grad, "seq", axis=0, tiled=True)
    piece_log = lax.all_gather(log_total, "seq", axis=0, tiled=True)
    piece_delta = lax.all_gather(row_delta, "seq", axis=0, tiled=True)
    piece_count = piece_q.shape[0]
    sub_rows = math.gcd(piece_count, 1024)

    def sub_step(sub_id, inner_carry):
        grad_k, grad_v = inner_carry
        offset = sub_id * sub_rows
        query_block = lax.dynamic_slice_in_dim(piece_q, offset, sub_rows, 0).astype(jnp.bfloat16)
        grad_rows = lax.dynamic_slice_in_dim(piece_grad, offset, sub_rows, 0).astype(jnp.bfloat16)
        log_block = lax.dynamic_slice_in_dim(piece_log, offset, sub_rows, 0)
        delta_block = lax.dynamic_slice_in_dim(piece_delta, offset, sub_rows, 0)
        scores = cross(query_block, rot_k) * score_scale
        weights = jnp.exp(scores - log_block[:, None])
        grad_w = cross(grad_rows, plain_v)
        grad_s = (weights * (grad_w - delta_block[:, None])).astype(jnp.bfloat16)
        grad_k = grad_k + inner(grad_s, query_block) * score_scale
        grad_v = grad_v + inner(weights.astype(jnp.bfloat16), grad_rows)
        return (grad_k, grad_v)

    grad_k, grad_v = lax.fori_loop(0, piece_count // sub_rows, sub_step, fold_start)
    grad_queries = rotate(grad_q, cos_table, sin_table, -1.0).astype(jnp.bfloat16)[:, None, :]
    grad_keys = rotate(grad_k, cos_table, sin_table, -1.0).astype(jnp.bfloat16)[:, None, :]
    grad_values = grad_v.astype(jnp.bfloat16)[:, None, :]
    return (grad_queries, grad_keys, grad_values)


def solution(mesh):
    in_specs = (
        P(("dp", "seq"), "tm", None),
        P(("dp", "seq"), "tm", None),
        P(("dp", "seq"), "tm", None),
        P("seq"),
        P("tm", None, None),
        P(),
        P(),
        P("dp"),
        P(("dp", "tm"), "seq", None),
    )
    out_specs = (
        P(("dp", "seq"), "tm", None),
        P(("dp", "seq"), "tm", None),
        P(("dp", "seq"), "tm", None),
    )
    return jax.shard_map(
        on_device, mesh=mesh, in_specs=in_specs, out_specs=out_specs, check_vma=False
    )
```

profile of v0, /device:TPU:4, one launch (start us, length us, event | category | flops | bytes accessed | tf_op | source)
XLA Modules:
  0.0 426.8 jit_solution(6514035259708986628)
XLA Ops:
  13.6 73.2 %all-gather.8.cloned.1.call-done = bf16[8192,128]{0,1:T(8,128)(2,1)} async-done(((bf16[512,128]{0,1:T(8,128)(2,1)}), bf16[8192,128]{0,1:T(8,128)(2,1)}) %all-gather.8.cloned.1.call-update) | async-done | bytes 2097168 | tf_op jit(solution)/shard_map/all_gather | solution.py:91
  86.8 4.1 copy.61
  90.9 66.2 %all-gather.14.cloned.1.call-done = bf16[8192,1,128]{2,0,1:T(8,128)(2,1)} async-done(((bf16[512,1,128]{2,0,1:T(8,128)(2,1)}), bf16[8192,1,128]{2,0,1:T(8,128)(2,1)}) %all-gather.14.cloned.1.call-update) | async-done | bytes 2097168 | tf_op jit(solution)/shard_map/all_gather | solution.py:92
  157.2 26.8 %while.48 = (s32[]{:T(128)}, f32[512]{0:T(512)S(1)}, f32[512]{0:T(512)S(1)}, f32[512,128]{1,0:T(8,128)S(1)}, bf16[8192,128]{1,0:T(8,128)(2,1)}, /*index=5*/bf16[...) while((s32[]{:T(128)}, f32[512]{0:T(512)S(1)}, ...), condition=%wide.region_3.4_spmd.clone, body=%wide.region_0.3_spmd.clone.sunk | while | flops 272828928 | bytes 7504047 | solution.py:117
  190.8 34.3 %all-gather.1 = f32[16,1,512]{2,1,0:T(1,128)} all-gather(f32[1,1,512]{2,1,0:T(1,128)S(1)} %bitcast.108), channel_id=1, replica_groups=mesh['seq'=16,'tm'=8,'dp'=2] {'seq'}, dimensions={0}, use_global_device_ids=true | all-gather | bytes 34816 | tf_op jit(solution)/shard_map/all_gather | solution.py:181
  228.3 11.8 %all_gather.23 = bf16[512,384]{1,0:T(8,128)(2,1)S(1)} all-gather(bf16[64,384]{1,0:T(8,128)(2,1)S(1)} %bitcast.103), channel_id=1, replica_groups=mesh['seq'=16,'tm'=8,'dp'=2] {'tm'}, dimensions={0}, use_global_device_ids=true | all-gather | bytes 442368 | tf_op jit(solution)/shard_map/all_gather | solution.py:157
  241.6 35.1 %while.49 = (s32[]{:T(128)}, f32[512,128]{1,0:T(8,128)}, bf16[8192,128]{1,0:T(8,128)(2,1)}, bf16[512,128]{1,0:T(8,128)(2,1)S(1)}, f32[512]{0:T(512)}, /*index=5*...) while((s32[]{:T(128)}, f32[512,128]{1,0:T(8,128)}, ...), condition=%wide.region_9.10_spmd.clone, body=%wide.region_8.9_spmd.clone.sunk | while | flops 405471232 | bytes 7886624 | solution.py:175
  243.1 2.2 fusion.122
  247.5 2.2 fusion.122
  251.9 2.2 fusion.122
  256.3 2.2 fusion.122
  260.7 2.2 fusion.122
  269.4 2.2 fusion.122
  273.8 2.2 fusion.122
  278.0 32.2 %all-gather.2 = f32[16,1,512]{2,1,0:T(1,128)} all-gather(f32[1,1,512]{2,1,0:T(1,128)} %bitcast.109), channel_id=1, replica_groups=mesh['seq'=16,'tm'=8,'dp'=2] {'seq'}, dimensions={0}, use_global_device_ids=true | all-gather | bytes 34816 | tf_op jit(solution)/shard_map/all_gather | solution.py:182
  311.0 48.9 %all-gather.12.cloned.1.call-done = bf16[8192,128]{0,1:T(8,128)(2,1)} async-done(((bf16[512,128]{0,1:T(8,128)(2,1)}), bf16[8192,128]{0,1:T(8,128)(2,1)}) %all-gather.12.cloned.1.call-update) | async-done | bytes 2097168 | tf_op jit(solution)/shard_map/all_gather | solution.py:180
  359.9 54.8 %while.50 = (s32[]{:T(128)}, f32[512,128]{1,0:T(8,128)}, f32[512,128]{1,0:T(8,128)S(1)}, bf16[8192,128]{0,1:T(8,128)(2,1)}, bf16[512,128]{1,0:T(8,128)(2,1)S(1)}...) while((s32[]{:T(128)}, f32[512,128]{1,0:T(8,128)}, ...), condition=%wide.region_11.12_spmd.clone, body=%wide.region_10.11_spmd.clone.sunk | while | flops 541392896 | bytes 11301086 | solution.py:201
  370.0 2.9 fusion.131
  376.9 2.9 fusion.131
  383.9 2.9 fusion.131
  390.9 2.9 fusion.131
  397.8 2.9 fusion.131
  404.8 2.9 fusion.131
  411.8 2.9 fusion.131
  (306 shorter events, 105.1 us)
Async XLA Ops:
  7.2 177.0 %copy-start = (bf16[1,128,384]{2,1,0:T(8,128)(2,1)S(1)}, bf16[1,128,384]{2,1,0:T(8,128)(2,1)}, u32[]{:S(2)}) copy-start(bf16[1,128,384]{2,1,0:T(8,128)(2,1)} %param.19) | copy-start | bytes 294916
  7.2 79.6 %all-gather.8.cloned.1.call-start = ((), (), s32[]{:S(2)}) async-start(), calls=%async_computation.1 | async-start | bytes 2228224 | tf_op jit(solution)/shard_map/all_gather | solution.py:91
  10.9 80.0 %copy-start.6 = (f32[512,21,1]{0,1,2:T(8,128)}, f32[512,21,1]{0,1,2:T(8,128)S(1)}, u32[]{:S(2)}) copy-start(f32[512,21,1]{0,1,2:T(8,128)S(1)} %get-tuple-element.690) | copy-start | bytes 129028
  10.9 80.0 %copy-start.7 = (f32[512,21,1]{0,1,2:T(8,128)}, f32[512,21,1]{0,1,2:T(8,128)S(1)}, u32[]{:S(2)}) copy-start(f32[512,21,1]{0,1,2:T(8,128)S(1)} %get-tuple-element.691) | copy-start | bytes 129028
  12.4 144.7 %all-gather.14.cloned.1.call-start = ((), (), s32[]{:S(2)}) async-start(), calls=%async_computation.5 | async-start | bytes 2228224 | tf_op jit(solution)/shard_map/all_gather | solution.py:92
  13.2 212.0 %reduce-scatter.2.cloned.1.call-start = ((), (), s32[]{:S(2)}) async-start(), calls=%async_computation.2 | async-start | bytes 442368 | tf_op jit(solution)/shard_map/reduce_scatter | solution.py:122
  13.4 77.5 %copy-start.2 = (bf16[512,128]{0,1:T(8,128)(2,1)}, bf16[512,128]{0,1:T(8,128)(2,1)S(1)}, u32[]{:S(2)}) copy-start(bf16[512,128]{0,1:T(8,128)(2,1)S(1)} %convert_element_type.145) | copy-start | bytes 393220
  184.0 6.8 %copy-start.12 = (f32[512]{0:T(512)}, f32[512]{0:T(512)S(1)}, u32[]{:S(2)}) copy-start(f32[512]{0:T(512)S(1)} %get-tuple-element.424) | copy-start | bytes 6148
  184.0 3.9 copy-start.1
  184.0 6.0 %copy-start.4 = (bf16[3,384,768]{2,1,0:T(8,128)(2,1)S(1)}, bf16[3,384,768]{2,1,0:T(8,128)(2,1)}, u32[]{:S(2)}) copy-start(bf16[3,384,768]{2,1,0:T(8,128)(2,1)} %param.21) | copy-start | bytes 5308420
  184.1 6.2 %copy-start.3 = (bf16[512,128]{0,1:T(8,128)(2,1)S(1)}, bf16[512,128]{0,1:T(8,128)(2,1)}, u32[]{:S(2)}) copy-start(bf16[512,128]{0,1:T(8,128)(2,1)} %convert_element_type.142) | copy-start | bytes 393220
  185.2 41.8 %copy-start.17 = (f32[384]{0:T(512)S(1)}, f32[384]{0:T(512)}, u32[]{:S(2)}) copy-start(f32[384]{0:T(512)} %param.20) | copy-start | bytes 4612
  185.3 125.7 %all-gather.10.cloned.1.call-start = ((), (), s32[]{:S(2)}) async-start(), calls=%async_computation.3 | async-start | bytes 2228224 | tf_op jit(solution)/shard_map/all_gather | solution.py:179
  185.8 174.1 %all-gather.12.cloned.1.call-start = ((), (), s32[]{:S(2)}) async-start(), calls=%async_computation.4 | async-start | bytes 2228224 | tf_op jit(solution)/shard_map/all_gather | solution.py:180
  185.9 4.6 %collective-permute-start = (bf16[2,32,768]{2,1,0:T(8,128)(2,1)S(1)}, bf16[2,32,768]{2,1,0:T(8,128)(2,1)S(1)}, u32[]{:S(2)}, u32[]{:S(2)}) collective-permute-start(bf16[2,32,768]{2,1,0:T(8,128)(2,1)S(1)} %copy-done.11), channel_id=1, source_target_pairs={{2,0},{4,2},{6,4},{8,6},{10,8},{12,10},{14,12},{3,1},{5,3},{7,5},{... | collective-permute-start | bytes 294920 | tf_op jit(solution)/shard_map/ppermute | solution.py:14
  190.8 36.2 %copy-start.14 = (f32[512]{0:T(512)}, f32[512]{0:T(512)S(1)}, u32[]{:S(2)}) copy-start(f32[512]{0:T(512)S(1)} %log_add_fusion) | copy-start | bytes 6148
  190.8 49.3 %copy-start.13 = (f32[512]{0:T(512)S(1)}, f32[512]{0:T(512)}, u32[]{:S(2)}) copy-start(f32[512]{0:T(512)} %copy-done.12) | copy-start | bytes 6148
  367.8 2.2 copy-start.10
  374.7 2.2 copy-start.10
  381.7 2.2 copy-start.10
  388.7 2.2 copy-start.10
  395.6 2.2 copy-start.10
  402.6 2.2 copy-start.10
  409.6 2.2 copy-start.10
  (35 other events, 45.4 us)
Sparse Core Ops, SparseCore 0:
  12.5 74.2 all-gather.7
  88.6 68.5 all-gather.13
  185.4 26.1 reduce-scatter.1
  213.8 75.1 all-gather.9
  291.2 68.6 all-gather.11
where the time goes:
time: 429 us; the launch traced here: 427 us
  waiting for transfers between devices  190 us (44%)
  matrix products  86.8 us (20%)
  blocking collectives  78.3 us (18%)
  local copies, waits for them, and re-layouts  45.6 us (11%)
  between operations  14.3 us (3%)
  other arithmetic  9.06 us (2%)
    all_gather x1, waiting for transfers between devices, on_device(): lax.all_gather(rot_k, 'seq', axis=0, tiled=True)  73.2 us
    all_gather x1, waiting for transfers between devices, on_device(): lax.all_gather(plain_v, 'seq', axis=0, tiled=True)  66.2 us
    all_gather x1, waiting for transfers between devices, on_device(): piece_grad = lax.all_gather(wide_grad, 'seq', axis=0, tiled=True)  48.9 us
    all_gather x1, blocking collectives, on_device(): piece_log = lax.all_gather(log_total, 'seq', axis=0, tiled=True)  34.3 us
    all_gather x1, blocking collectives, on_device(): piece_delta = lax.all_gather(row_delta, 'seq', axis=0, tiled=True)  32.2 us
    dot_general x16, matrix products, inner(): lax.dot_general(left, right, (((0,), (0,)), ((), ())), preferred_element_...  28.5 us
    dot_general x25, matrix products, cross(): lax.dot_general(left, right, (((1,), (1,)), ((), ())), preferred_element_...  26.9 us
    dot_general x8, matrix products, query_step(): jnp.dot(grad_s, key_piece, preferred_element_type=jnp.float32) * score_scale  17.4 us
  transfers between devices with their start and end apart: 6, of which 3 were waited for; matrix products, arithmetic and copies ran while one was open for 10% of the time, Pallas kernels for 0%

commit v1 on v0

--- a/solution.py
+++ b/solution.py
@@ -89,7 +89,9 @@
     plain_v = values[:, 0, :]
     keys_all, values_all = (
         lax.all_gather(rot_k, "seq", axis=0, tiled=True),
-        lax.all_gather(plain_v, "seq", axis=0, tiled=True),
+        jnp.concatenate(
+            lax.all_to_all(jnp.stack([plain_v] * lax.axis_size("seq")), "seq", 0, 0), axis=0
+        ),
     )
     total_tokens = keys_all.shape[0]
     key_block = math.gcd(total_tokens, 1024)

time: 429 us -> 386 us (0.90)
  waiting for transfers between devices: 190 us -> 142 us
  starting transfers between devices: 2.12 us -> 11.7 us
  local copies, waits for them, and re-layouts: 45.6 us -> 40.6 us
    all_gather x1 -> x0, waiting for transfers between devices: 66.2 us -> none  [on_device(): lax.all_gather(plain_v, 'seq', axis=0, tiled=True)]
    all_gather x1, waiting for transfers between devices: 73.2 us -> 84.1 us  [on_device(): lax.all_gather(rot_k, 'seq', axis=0, tiled=True)]
    all_to_all x0 -> x1, starting transfers between devices: none -> 9.63 us  [on_device(): lax.all_to_all(jnp.stack([plain_v] * lax.axis_size('seq')), 'seq', 0, 0)]
    all_gather x1, waiting for transfers between devices: 48.9 us -> 57.1 us  [on_device(): piece_grad = lax.all_gather(wide_grad, 'seq', axis=0, tiled=True)]
    while x88 -> x24, local copies, waits for them, and re-layouts: 5.89 us -> 0.07 us
  transfers between devices with their start and end apart: 6 -> 6, of which waited for: 3 -> 2; matrix products, arithmetic and copies ran while one was open for 10% -> 11% of each run, Pallas kernels for 0% -> 0%
where the time goes in v1:
time: 386 us; the launch traced here: 384 us
  waiting for transfers between devices  142 us (37%)
  matrix products  86 us (22%)
  blocking collectives  79.1 us (20%)
  local copies, waits for them, and re-layouts  40.6 us (11%)
  between operations  14.3 us (4%)
  starting transfers between devices  11.7 us (3%)
  other arithmetic  9.06 us (2%)
    all_gather x1, waiting for transfers between devices, on_device(): lax.all_gather(rot_k, 'seq', axis=0, tiled=True)  84.1 us
    all_gather x1, waiting for transfers between devices, on_device(): piece_grad = lax.all_gather(wide_grad, 'seq', axis=0, tiled=True)  57.1 us
    all_gather x1, blocking collectives, on_device(): piece_log = lax.all_gather(log_total, 'seq', axis=0, tiled=True)  35.1 us
    all_gather x1, blocking collectives, on_device(): piece_delta = lax.all_gather(row_delta, 'seq', axis=0, tiled=True)  32.2 us
    dot_general x16, matrix products, inner(): lax.dot_general(left, right, (((0,), (0,)), ((), ())), preferred_element_...  28.7 us
    dot_general x25, matrix products, cross(): lax.dot_general(left, right, (((1,), (1,)), ((), ())), preferred_element_...  26 us
    dot_general x8, matrix products, query_step(): jnp.dot(grad_s, key_piece, preferred_element_type=jnp.float32) * score_scale  17.4 us
    dot_general x8, matrix products, forward_step(): jnp.dot(weights.astype(jnp.bfloat16), value_piece, preferred_element_type...  11.9 us
  transfers between devices with their start and end apart: 6, of which 2 were waited for; matrix products, arithmetic and copies ran while one was open for 11% of the time, Pallas kernels for 0%

profile of v1, /device:TPU:4, one launch (start us, length us, event | category | flops | bytes accessed | tf_op | source)
XLA Modules:
  0.0 383.6 jit_solution(14783803015154764872)
XLA Ops:
  14.2 9.6 %all-to-all-start = ((bf16[16,512,128]{2,1,0:T(8,128)(2,1)}), bf16[16,512,128]{2,1,0:T(8,128)(2,1)}, u32[]{:S(2)}, u32[]{:S(2)}) async-start(bf16[16,512,128]{2,1,0:T(8,128)(2,1)} %stack.47), calls=%async_computation | async-start | bytes 4194304 | tf_op jit(solution)/shard_map/all_to_all | solution.py:93
  24.2 84.1 %all-gather.6.cloned.1.call-done = bf16[8192,128]{0,1:T(8,128)(2,1)} async-done(((bf16[512,128]{0,1:T(8,128)(2,1)}), bf16[8192,128]{0,1:T(8,128)(2,1)}) %all-gather.6.cloned.1.call-update) | async-done | bytes 2097168 | tf_op jit(solution)/shard_map/all_gather | solution.py:91
  108.4 4.1 %copy.61 = bf16[8192,128]{1,0:T(8,128)(2,1)} copy(bf16[8192,128]{0,1:T(8,128)(2,1)} %all-gather.6.cloned.1.call-done) | data formatting | bytes 4194304
  112.5 26.8 %while.48 = (s32[]{:T(128)}, f32[512]{0:T(512)S(1)}, f32[512]{0:T(512)S(1)}, f32[512,128]{1,0:T(8,128)S(1)}, bf16[8192,128]{1,0:T(8,128)(2,1)}, /*index=5*/bf16[...) while((s32[]{:T(128)}, f32[512]{0:T(512)S(1)}, ...), condition=%wide.region_3.4_spmd.clone, body=%wide.region_0.3_spmd.clone.sunk | while | flops 272828928 | bytes 7504047 | solution.py:119
  146.3 35.1 %all-gather = f32[16,1,512]{2,1,0:T(1,128)} all-gather(f32[1,1,512]{2,1,0:T(1,128)S(1)} %bitcast.108), channel_id=1, replica_groups=mesh['seq'=16,'tm'=8,'dp'=2] {'seq'}, dimensions={0}, use_global_device_ids=true | all-gather | bytes 34816 | tf_op jit(solution)/shard_map/all_gather | solution.py:183
  184.6 11.8 %all_gather.19 = bf16[512,384]{1,0:T(8,128)(2,1)S(1)} all-gather(bf16[64,384]{1,0:T(8,128)(2,1)S(1)} %bitcast.102), channel_id=1, replica_groups=mesh['seq'=16,'tm'=8,'dp'=2] {'tm'}, dimensions={0}, use_global_device_ids=true | all-gather | bytes 442368 | tf_op jit(solution)/shard_map/all_gather | solution.py:159
  197.3 28.8 %while.49 = (s32[]{:T(128)}, f32[512,128]{1,0:T(8,128)S(1)}, bf16[8192,128]{1,0:T(8,128)(2,1)}, bf16[512,128]{1,0:T(8,128)(2,1)S(1)}, f32[512]{0:T(512)S(1)}, /*...) while((s32[]{:T(128)}, f32[512,128]{1,0:T(8,128)S(1)}, ...), condition=%wide.region_9.10_spmd.clone, body=%wide.region_8.9_spmd.clone.sunk | while | flops 405471232 | bytes 5772976 | solution.py:177
  198.7 2.2 fusion.122
  202.3 2.2 fusion.122
  205.9 2.2 fusion.122
  209.5 2.2 fusion.122
  213.1 2.2 fusion.122
  216.7 2.2 fusion.122
  220.3 2.2 fusion.122
  226.4 32.2 %all-gather.1 = f32[16,1,512]{2,1,0:T(1,128)} all-gather(f32[1,1,512]{2,1,0:T(1,128)S(1)} %bitcast.109), channel_id=1, replica_groups=mesh['seq'=16,'tm'=8,'dp'=2] {'seq'}, dimensions={0}, use_global_device_ids=true | all-gather | bytes 34816 | tf_op jit(solution)/shard_map/all_gather | solution.py:184
  259.4 57.1 %all-gather.10.cloned.1.call-done = bf16[8192,128]{0,1:T(8,128)(2,1)} async-done(((bf16[512,128]{0,1:T(8,128)(2,1)}), bf16[8192,128]{0,1:T(8,128)(2,1)}) %all-gather.10.cloned.1.call-update) | async-done | bytes 2097168 | tf_op jit(solution)/shard_map/all_gather | solution.py:182
  316.5 55.0 %while.50 = (s32[]{:T(128)}, f32[512,128]{1,0:T(8,128)}, f32[512,128]{1,0:T(8,128)S(1)}, bf16[8192,128]{0,1:T(8,128)(2,1)}, bf16[512,128]{1,0:T(8,128)(2,1)S(1)}...) while((s32[]{:T(128)}, f32[512,128]{1,0:T(8,128)}, ...), condition=%wide.region_11.12_spmd.clone, body=%wide.region_10.11_spmd.clone.sunk | while | flops 541392896 | bytes 11301086 | solution.py:203
  326.6 2.9 fusion.131
  333.6 2.9 fusion.131
  340.6 2.9 fusion.131
  347.6 2.9 fusion.131
  354.6 2.9 fusion.131
  361.5 2.9 fusion.131
  368.5 2.9 fusion.131
  (238 shorter events, 98.7 us)
Async XLA Ops:
  7.2 132.3 %copy-start = (bf16[1,128,384]{2,1,0:T(8,128)(2,1)S(1)}, bf16[1,128,384]{2,1,0:T(8,128)(2,1)}, u32[]{:S(2)}) copy-start(bf16[1,128,384]{2,1,0:T(8,128)(2,1)} %param.19) | copy-start | bytes 294916
  7.2 101.2 %all-gather.6.cloned.1.call-start = ((), (), s32[]{:S(2)}) async-start(), calls=%async_computation.2 | async-start | bytes 2228224 | tf_op jit(solution)/shard_map/all_gather | solution.py:91
  9.2 3.3 copy-start.8
  11.0 0.6 copy-start.7
  14.2 98.3 %all-to-all-start = ((bf16[16,512,128]{2,1,0:T(8,128)(2,1)}), bf16[16,512,128]{2,1,0:T(8,128)(2,1)}, u32[]{:S(2)}, u32[]{:S(2)}) async-start(bf16[16,512,128]{2,1,0:T(8,128)(2,1)} %stack.47), calls=%async_computation | async-start | bytes 4194304 | tf_op jit(solution)/shard_map/all_to_all | solution.py:93
  23.8 157.6 %reduce-scatter.2.cloned.1.call-start = ((), (), s32[]{:S(2)}) async-start(), calls=%async_computation.3 | async-start | bytes 442368 | tf_op jit(solution)/shard_map/reduce_scatter | solution.py:124
  24.1 88.4 %copy-start.2 = (bf16[512,128]{0,1:T(8,128)(2,1)}, bf16[512,128]{0,1:T(8,128)(2,1)S(1)}, u32[]{:S(2)}) copy-start(bf16[512,128]{0,1:T(8,128)(2,1)S(1)} %convert_element_type.145) | copy-start | bytes 393220
  139.3 2.0 copy-start.10
  139.3 4.0 %copy-start.1 = (s32[16]{0:T(128)S(1)}, s32[16]{0:T(128)}, u32[]{:S(2)}) copy-start(s32[16]{0:T(128)} %param.22) | copy-start | bytes 196
  139.4 6.1 %copy-start.4 = (bf16[3,384,768]{2,1,0:T(8,128)(2,1)S(1)}, bf16[3,384,768]{2,1,0:T(8,128)(2,1)}, u32[]{:S(2)}) copy-start(bf16[3,384,768]{2,1,0:T(8,128)(2,1)} %param.21) | copy-start | bytes 5308420
  139.5 6.3 %copy-start.3 = (bf16[512,128]{0,1:T(8,128)(2,1)S(1)}, bf16[512,128]{0,1:T(8,128)(2,1)}, u32[]{:S(2)}) copy-start(bf16[512,128]{0,1:T(8,128)(2,1)} %convert_element_type.142) | copy-start | bytes 393220
  140.6 42.7 %copy-start.11 = (f32[384]{0:T(512)S(1)}, f32[384]{0:T(512)}, u32[]{:S(2)}) copy-start(f32[384]{0:T(512)} %param.20) | copy-start | bytes 4612
  140.6 118.9 %all-gather.8.cloned.1.call-start = ((), (), s32[]{:S(2)}) async-start(), calls=%async_computation.4 | async-start | bytes 2228224 | tf_op jit(solution)/shard_map/all_gather | solution.py:181
  141.3 175.2 %all-gather.10.cloned.1.call-start = ((), (), s32[]{:S(2)}) async-start(), calls=%async_computation.5 | async-start | bytes 2228224 | tf_op jit(solution)/shard_map/all_gather | solution.py:182
  141.4 4.6 %collective-permute-start = (bf16[2,32,768]{2,1,0:T(8,128)(2,1)S(1)}, bf16[2,32,768]{2,1,0:T(8,128)(2,1)S(1)}, u32[]{:S(2)}, u32[]{:S(2)}) collective-permute-start(bf16[2,32,768]{2,1,0:T(8,128)(2,1)S(1)} %copy-done.10), channel_id=1, source_target_pairs={{2,0},{4,2},{6,4},{8,6},{10,8},{12,10},{14,12},{3,1},{5,3},{7,5},{... | collective-permute-start | bytes 294920 | tf_op jit(solution)/shard_map/ppermute | solution.py:14
  196.6 0.7 copy-start.5
  318.3 2.2 copy-start.9
  324.4 2.2 copy-start.9
  331.4 2.2 copy-start.9
  338.4 2.2 copy-start.9
  345.3 2.2 copy-start.9
  352.3 2.2 copy-start.9
  359.3 2.2 copy-start.9
  366.3 2.2 copy-start.9
  (1 other events, 0.6 us)
Sparse Core Ops, SparseCore 0:
  12.6 95.7 all-gather.5
  140.7 27.0 reduce-scatter.1
  170.2 75.2 all-gather.7
  247.7 68.6 all-gather.9
